TPU v7x, 512 devices: a whole 4x8x8 slice. The times are simulated.
512 devices in a mesh: rows: 32 (over y, x), vocab: 16 (over z, core).
Axes of the slice: x: 4, y: 8, z: 8, core: 2. Of those that a mesh axis runs over, the one named last changes fastest.
Arguments:
- hidden: bfloat16 [12288, 8192], P('rows', 'vocab'), may hold values from -128 to 128
- head: bfloat16 [8192, 8192], P('rows', 'vocab'), may hold values from -4 to 4
- targets: int32 [12288], P('rows'), may hold values from 0 to 128255
- live: int32 [12288], P('rows'), may hold values from 0 to 1, as said below
- prior_lse: float32 [12288], P('rows'), may hold values from 10 to 18
- prior_mean: float32 [12288], P('rows'), may hold values from 2 to 8
- prior_target: float32 [12288], P('rows'), may hold values from -12 to 12
- seq_lengths: int32 [32], replicated, may hold values from 1 to 768, 12288 in all
Outputs:
- logprob: float32 [12288], P(('rows', 'vocab'))
- entropy: float32 [12288], P(('rows', 'vocab'))
- seq_score: float32 [32], replicated
Inputs may be any that keep to these rules, and one draw needn't show every extreme that they name: Within the 384 rows of each index of rows, the live rows come first; every such index has at least 48 live rows and some index has all 384.
All inputs are finite; a program needn't handle non-finite values.
Results may differ from a plain program's by a relative error of at most 0.0003.
Values may be sent and summed in bfloat16 or wider, within the bound.
No kernel may reach another device: no remote copies, remote signals or barrier semaphores. Data moves between devices by JAX's collectives and lax.ppermute only.
A program may use at most 64 MiB of HBM per device.

v0:
```python
import jax
import jax.numpy as jnp
from jax import lax
from jax.sharding import PartitionSpec as P

VOCAB = 128256
SEQS = 32
GSIZE = 8


def finish_rows(block_peak, block_mass, block_moment, block_target, live, prior_lse, prior_mean):
    highest = jnp.maximum(block_peak, prior_lse)
    earlier = jnp.exp(prior_lse - highest)
    scaled = jnp.exp(block_peak - highest)
    total_mass = earlier + block_mass * scaled
    norm_log = highest + jnp.log(total_mass)
    average = (earlier * prior_mean + scaled * block_moment) / total_mass
    keeping = live.astype(jnp.float32)
    return (keeping * (block_target - norm_log), keeping * (norm_log - average))


def local(hidden, head, targets, live, prior_lse, prior_mean, prior_target, seq_lengths):
    rows_here = hidden.shape[0]
    cols_here = head.shape[1]
    spread = lax.axis_size("vocab")
    which = lax.axis_index("vocab")
    block_first = VOCAB - cols_here * spread
    first_col = block_first + which * cols_here
    gathered = lax.all_gather(hidden, "vocab", axis=1, tiled=True)
    logits = jnp.dot(
        gathered,
        lax.all_gather(head, "rows", axis=0, tiled=True),
        preferred_element_type=jnp.float32,
    )
    row_peak = jnp.max(logits, axis=1)
    weights = jnp.exp(logits - row_peak[:, None])
    row_mass = jnp.sum(weights, axis=1)
    moment = jnp.sum(weights * logits, axis=1)
    column = targets - first_col
    columns = lax.broadcasted_iota(jnp.int32, logits.shape, 1)
    picked = jnp.sum(jnp.where(columns == column[:, None], logits, jnp.zeros_like(logits)), axis=1)
    stats = jnp.stack([row_peak, row_mass, moment, picked])
    every = lax.all_gather(stats, "vocab", axis=0, tiled=False)
    peaks = every[:, 0]
    highest = jnp.max(peaks, axis=0)
    factor = jnp.exp(peaks - highest[None, :])
    mass_all = jnp.sum(every[:, 1] * factor, axis=0)
    moment_all = jnp.sum(every[:, 2] * factor, axis=0)
    picked_all = jnp.sum(every[:, 3], axis=0)
    block_target = jnp.where(targets >= block_first, picked_all, prior_target)
    logprob, entropy = finish_rows(
        highest, mass_all, moment_all, block_target, live, prior_lse, prior_mean
    )
    share = rows_here // spread
    begin = which * share
    logprob_share = lax.dynamic_slice_in_dim(logprob, begin, share, 0)
    entropy_share = lax.dynamic_slice_in_dim(entropy, begin, share, 0)
    global_rows = lax.axis_index("rows") * rows_here + jnp.arange(rows_here, dtype=jnp.int32)
    endings = jnp.cumsum(seq_lengths)
    member = jnp.sum((global_rows[:, None] >= endings[None, :]).astype(jnp.int32), axis=1)
    onehot = (member[:, None] == jnp.arange(SEQS, dtype=jnp.int32)[None, :]).astype(jnp.float32)
    partial_sums = jnp.sum(onehot * logprob[:, None], axis=0)
    sums = jnp.sum(lax.all_gather(partial_sums, "rows", axis=0, tiled=False), axis=0)
    seq_mean = sums / seq_lengths.astype(jnp.float32)
    grouped = seq_mean.reshape(SEQS // GSIZE, GSIZE)
    seq_score = (grouped - jnp.mean(grouped, axis=1, keepdims=True)).reshape(SEQS)
    return (logprob_share, entropy_share, seq_score)


def solution(mesh):
    return jax.shard_map(
        local,
        mesh=mesh,
        in_specs=(
            P("rows", "vocab"),
            P("rows", "vocab"),
            P("rows"),
            P("rows"),
            P("rows"),
            P("rows"),
            P("rows"),
            P(),
        ),
        out_specs=(P(("rows", "vocab")), P(("rows", "vocab")), P()),
        check_vma=False,
    )
```

profile of v0, /device:TPU:2, one launch (start us, length us, event | category | flops | bytes accessed | tf_op | source)
XLA Modules:
  0.0 275.6 jit_solution(6936003982868174059)
XLA Ops:
  7.2 0.7 all-gather.6.cloned.1.call-update
  7.9 0.7 all-gather.8.cloned.1.call-update
  8.7 0.7 copy.22
  9.5 0.1 reduce.2
  9.6 1.3 dynamic-slice
  11.5 0.1 convert_reduce_fusion
  11.6 0.7 broadcast_subtract_fusion
  12.3 52.0 %all-gather.6.cloned.1.call-done = bf16[384,8192]{1,0:T(8,128)(2,1)} async-done(((bf16[384,512]{1,0:T(8,128)(2,1)}), bf16[384,8192]{1,0:T(8,128)(2,1)}) %all-gather.6.cloned.1.call-update) | async-done | bytes 6291472 | tf_op jit(solution)/shard_map/all_gather | solution.py:29
  64.3 103.5 %all-gather.8.cloned.1.call-done = bf16[8192,512]{1,0:T(8,128)(2,1)} async-done(((bf16[256,512]{1,0:T(8,128)(2,1)}), bf16[8192,512]{1,0:T(8,128)(2,1)}) %all-gather.8.cloned.1.call-update) | async-done | bytes 8388624 | tf_op jit(solution)/shard_map/all_gather | solution.py:32
  167.7 8.0 %fusion.7 = (f32[384]{0:T(512)S(1)}, f32[384,512]{1,0:T(8,128)S(1)}) fusion(bf16[384,8192]{1,0:T(8,128)(2,1)} %all-gather.6.cloned.1.call-done, bf16[8192,512]{1,0:T(8,128)(2,1)} %all-gather.8.cloned.1.call-done), kind=kOutput, calls=%fused_computation.30 | convolution fusion | flops 3221421568 | bytes 15468032 | tf_op jit(solution)/shard_map/dot_general | solution.py:30
  175.8 0.5 fusion
  176.3 18.3 %all-gather.2 = f32[16,4,384]{2,1,0:T(4,128)S(1)} all-gather(f32[1,4,384]{2,1,0:T(4,128)S(1)} %maximum_bitcast_fusion), channel_id=2, replica_groups=mesh['rows'=32,'vocab'=16] {'vocab'}, dimensions={0}, use_global_device_ids=true | all-gather | bytes 104448 | tf_op jit(solution)/shard_map/all_gather | solution.py:43
  194.6 0.1 fusion.6
  194.8 0.6 dynamic_slice.6
  195.4 0.6 dynamic_slice.7
  196.0 0.1 select_reduce_fusion.1
  196.1 0.2 dynamic-update-slice
  196.4 71.4 %all-reduce = f32[1024]{0:T(1024)S(1)} all-reduce(f32[1024]{0:T(1024)S(1)} %dynamic-update-slice), channel_id=3, replica_groups=mesh['rows'=32,'vocab'=16] {'rows'}, use_global_device_ids=true, to_apply=%add | all-reduce | flops 1024 | bytes 8192
  267.8 0.1 reshape.52
  267.9 0.1 reshape.50
  268.0 0.1 reduce_sum.99
  268.1 0.1 sub.55
  268.2 0.1 sub.56
  268.2 0.5 sub.57
  (27 shorter events, 0.3 us)
Async XLA Ops:
  7.2 57.1 %all-gather.6.cloned.1.call-start = ((), (), s32[]{:S(2)}) async-start(), calls=%async_computation | async-start | bytes 6684672 | tf_op jit(solution)/shard_map/all_gather | solution.py:29
  7.9 159.8 %all-gather.8.cloned.1.call-start = ((), (), s32[]{:S(2)}) async-start(), calls=%async_computation.1 | async-start | bytes 8650752 | tf_op jit(solution)/shard_map/all_gather | solution.py:32
  12.3 182.5 %copy-start = (s32[384]{0:T(512)S(1)}, s32[384]{0:T(512)}, u32[]{:S(2)}) copy-start(s32[384]{0:T(512)} %param.10) | copy-start | bytes 4612
  12.3 182.5 %copy-start.1 = (f32[384]{0:T(512)S(1)}, f32[384]{0:T(512)}, u32[]{:S(2)}) copy-start(f32[384]{0:T(512)} %param.13) | copy-start | bytes 4612
  12.3 182.5 %copy-start.2 = (s32[384]{0:T(512)S(1)}, s32[384]{0:T(512)}, u32[]{:S(2)}) copy-start(s32[384]{0:T(512)} %param.11) | copy-start | bytes 4612
  12.3 182.5 %copy-start.3 = (f32[384]{0:T(512)S(1)}, f32[384]{0:T(512)}, u32[]{:S(2)}) copy-start(f32[384]{0:T(512)} %param.12) | copy-start | bytes 4612
  12.3 182.5 %copy-start.4 = (f32[384]{0:T(512)S(1)}, f32[384]{0:T(512)}, u32[]{:S(2)}) copy-start(f32[384]{0:T(512)} %param.14) | copy-start | bytes 4612
  12.3 255.5 %copy-start.5 = (s32[32]{0:T(128)S(1)}, s32[32]{0:T(128)}, u32[]{:S(2)}) copy-start(s32[32]{0:T(128)} %param.15) | copy-start | bytes 388
Sparse Core Ops, SparseCore 0:
  10.1 54.0 all-gather.5
  67.4 100.2 all-gather.7
where the time goes:
time: 276 us
  waiting for transfers between devices  157 us (57%)
  blocking collectives  89.7 us (32%)
  between operations  14.8 us (5%)
  matrix products  8 us (3%)
  local copies, waits for them, and re-layouts  3.78 us (1%)
    all_gather x1, waiting for transfers between devices, local(): lax.all_gather(head, 'rows', axis=0, tiled=True)  103 us
    unnamed x1, blocking collectives  71.4 us
    all_gather x1, waiting for transfers between devices, local(): gathered = lax.all_gather(hidden, 'vocab', axis=1, tiled=True)  52 us
    all_gather x1, blocking collectives, local(): every = lax.all_gather(stats, 'vocab', axis=0, tiled=False)  18.3 us
    dot_general x1, matrix products, local(): jnp.dot(gathered, lax.all_gather(head, 'rows', axis=0, tiled=True), prefe...  8 us
  transfers between devices with their start and end apart: 2, of which 2 were waited for; matrix products, arithmetic and copies ran while one was open for 1% of the time, Pallas kernels for 0%

commit v1 on v0

--- a/solution.py
+++ b/solution.py
@@ -29,7 +29,9 @@
     gathered = lax.all_gather(hidden, "vocab", axis=1, tiled=True)
     logits = jnp.dot(
         gathered,
-        lax.all_gather(head, "rows", axis=0, tiled=True),
+        jnp.concatenate(
+            lax.all_to_all(jnp.stack([head] * lax.axis_size("rows")), "rows", 0, 0), axis=0
+        ),
         preferred_element_type=jnp.float32,
     )
     row_peak = jnp.max(logits, axis=1)

time: 276 us -> 333 us (1.21)
  the two profiles are of different devices: /device:TPU:2 before, /device:TPU:32 now
where the time goes in v1:
time: 333 us; the launch traced here: 332 us
  waiting for transfers between devices  183 us (55%)
  blocking collectives  106 us (32%)
  between operations  14.8 us (4%)
  starting transfers between devices  10.3 us (3%)
  local copies, waits for them, and re-layouts  8.22 us (2%)
  matrix products  8.04 us (2%)
    all_to_all x1, waiting for transfers between devices, local(): lax.all_to_all(jnp.stack([head] * lax.axis_size('rows')), 'rows', 0, 0)  129 us
    unnamed x1, blocking collectives  83.6 us
    all_gather x1, waiting for transfers between devices, local(): gathered = lax.all_gather(hidden, 'vocab', axis=1, tiled=True)  53.4 us
    all_gather x1, blocking collectives, local(): every = lax.all_gather(stats, 'vocab', axis=0, tiled=False)  22.7 us
    all_to_all x1, starting transfers between devices, local(): lax.all_to_all(jnp.stack([head] * lax.axis_size('rows')), 'rows', 0, 0)  10.3 us
    dot_general x1, matrix products, local(): jnp.dot(gathered, jnp.concatenate(lax.all_to_all(jnp.stack([head] * lax.a...  8.04 us
  transfers between devices with their start and end apart: 2, of which 2 were waited for; matrix products, arithmetic and copies ran while one was open for 0% of the time, Pallas kernels for 0%

profile of v1, /device:TPU:32, one launch (start us, length us, event | category | flops | bytes accessed | tf_op | source)
XLA Modules:
  0.0 332.4 jit_solution(10693106749679313728)
XLA Ops:
  7.2 5.1 %stack.12 = bf16[32,256,512]{2,1,0:T(8,128)(2,1)} broadcast(bf16[256,512]{1,0:T(8,128)(2,1)} %param.9), dimensions={1,2} | broadcast | bytes 8650752 | tf_op jit(solution)/shard_map/stack | solution.py:33
  12.3 10.3 %all-to-all-start = ((bf16[32,256,512]{2,1,0:T(8,128)(2,1)}), bf16[32,256,512]{2,1,0:T(8,128)(2,1)}, u32[]{:S(2)}, u32[]{:S(2)}) async-start(bf16[32,256,512]{2,1,0:T(8,128)(2,1)} %stack.12), calls=%async_computation | async-start | bytes 16777216 | tf_op jit(solution)/shard_map/all_to_all | solution.py:33
  22.6 0.7 all-gather.5.cloned.1.call-update
  23.3 0.1 copy.22
  23.4 0.1 reduce.2
  23.6 1.3 dynamic-slice
  25.5 0.1 convert_reduce_fusion
  25.6 53.4 %all-gather.5.cloned.1.call-done = bf16[384,8192]{1,0:T(8,128)(2,1)} async-done(((bf16[384,512]{1,0:T(8,128)(2,1)}), bf16[384,8192]{1,0:T(8,128)(2,1)}) %all-gather.5.cloned.1.call-update) | async-done | bytes 6291472 | tf_op jit(solution)/shard_map/all_gather | solution.py:29
  79.0 128.8 %all-to-all-done = bf16[32,256,512]{2,1,0:T(8,128)(2,1)} async-done(((bf16[32,256,512]{2,1,0:T(8,128)(2,1)}), bf16[32,256,512]{2,1,0:T(8,128)(2,1)}, u32[]{:S(2)}, u32[]{:S(2)}) %all-to-all-start) | async-done | bytes 8388640 | tf_op jit(solution)/shard_map/all_to_all | solution.py:33
  207.9 8.0 %fusion.7 = (f32[384]{0:T(512)S(1)}, f32[384,512]{1,0:T(8,128)S(1)}) fusion(bf16[384,8192]{1,0:T(8,128)(2,1)} %all-gather.5.cloned.1.call-done, bf16[8192,512]{1,0:T(8,128)(2,1)} %bitcast), kind=kOutput, calls=%fused_computation.30 | convolution fusion | flops 3221421568 | bytes 15468032 | tf_op jit(solution)/shard_map/dot_general | solution.py:30
  215.9 0.5 fusion
  216.5 22.7 %all-gather.2 = f32[16,4,384]{2,1,0:T(4,128)S(1)} all-gather(f32[1,4,384]{2,1,0:T(4,128)S(1)} %maximum_bitcast_fusion), channel_id=2, replica_groups=mesh['rows'=32,'vocab'=16] {'vocab'}, dimensions={0}, use_global_device_ids=true | all-gather | bytes 104448 | tf_op jit(solution)/shard_map/all_gather | solution.py:45
  239.2 0.1 fusion.6
  239.4 0.1 select_reduce_fusion.1
  239.5 0.2 dynamic-update-slice
  239.8 83.6 %all-reduce = f32[1024]{0:T(1024)S(1)} all-reduce(f32[1024]{0:T(1024)S(1)} %dynamic-update-slice), channel_id=3, replica_groups=mesh['rows'=32,'vocab'=16] {'rows'}, use_global_device_ids=true, to_apply=%add | all-reduce | flops 1024 | bytes 8192
  323.4 0.1 reshape.58
  323.5 0.1 reshape.56
  323.6 0.1 reduce_sum.99
  323.7 0.1 sub.55
  323.8 0.1 sub.56
  323.8 0.5 sub.57
  324.4 0.6 dynamic_slice.6
  325.0 0.6 dynamic_slice.7
  (27 shorter events, 0.2 us)
Async XLA Ops:
  12.3 11.0 %copy-start.5 = (s32[32]{0:T(128)S(1)}, s32[32]{0:T(128)}, u32[]{:S(2)}) copy-start(s32[32]{0:T(128)} %param.15) | copy-start | bytes 388
  12.3 13.3 %copy-start = (s32[384]{0:T(512)S(1)}, s32[384]{0:T(512)}, u32[]{:S(2)}) copy-start(s32[384]{0:T(512)} %param.10) | copy-start | bytes 4612
  12.3 195.6 %all-to-all-start = ((bf16[32,256,512]{2,1,0:T(8,128)(2,1)}), bf16[32,256,512]{2,1,0:T(8,128)(2,1)}, u32[]{:S(2)}, u32[]{:S(2)}) async-start(bf16[32,256,512]{2,1,0:T(8,128)(2,1)} %stack.12), calls=%async_computation | async-start | bytes 16777216 | tf_op jit(solution)/shard_map/all_to_all | solution.py:33
  22.5 56.5 %all-gather.5.cloned.1.call-start = ((), (), s32[]{:S(2)}) async-start(), calls=%async_computation.1 | async-start | bytes 6684672 | tf_op jit(solution)/shard_map/all_gather | solution.py:29
  207.9 31.5 %copy-start.1 = (f32[384]{0:T(512)S(1)}, f32[384]{0:T(512)}, u32[]{:S(2)}) copy-start(f32[384]{0:T(512)} %param.13) | copy-start | bytes 4612
  207.9 31.5 %copy-start.2 = (s32[384]{0:T(512)S(1)}, s32[384]{0:T(512)}, u32[]{:S(2)}) copy-start(s32[384]{0:T(512)} %param.11) | copy-start | bytes 4612
  207.9 31.5 %copy-start.3 = (f32[384]{0:T(512)S(1)}, f32[384]{0:T(512)}, u32[]{:S(2)}) copy-start(f32[384]{0:T(512)} %param.12) | copy-start | bytes 4612
  207.9 31.5 %copy-start.4 = (f32[384]{0:T(512)S(1)}, f32[384]{0:T(512)}, u32[]{:S(2)}) copy-start(f32[384]{0:T(512)} %param.14) | copy-start | bytes 4612
Sparse Core Ops, SparseCore 0:
  25.5 53.4 all-gather.4
